TPU v7x, 256 devices: a whole 4x4x8 slice. The times are simulated.
256 devices in a mesh: cfg: 2 (over core), seq: 32 (over y, z_lo, x), rep: 4 (over z_hi).
Axes of the slice: x: 4, y: 4, z: 8 (z_hi: 4, z_lo: 2; z = z_hi * 2 + z_lo), core: 2. Of those that a mesh axis runs over, the one named last changes fastest.
Arguments:
- image_tokens: float32 [4, 4608, 1536], P('rep', 'seq')
- text_tokens: bfloat16 [2, 4, 160, 1536], P('cfg', 'rep', 'seq'), may hold values from -6 to 6
- mod_image: float32 [2, 4, 3, 1536], P('cfg', 'rep'), may hold values from -4 to 4
- mod_text: float32 [2, 4, 2, 1536], P('cfg', 'rep'), may hold values from -4 to 4
- text_lengths: int32 [2, 4], P('cfg', 'rep'), may hold values from 38 to 154, as said below
- item_group: int32 [4], P('rep'), may hold values from 0 to 3
- item_step: int32 [4], P('rep'), may hold values from 0 to 27
- step_sizes: float32 [28], replicated, may hold values from 0.05 to 0.4
- guide_scales: float32 [4], replicated, may hold values from 1.5 to 7
- qkv_weight: bfloat16 [1536, 2304], P(('cfg', 'seq', 'rep'))
- kv_weight: bfloat16 [1536, 1536], P(('cfg', 'seq', 'rep')), may hold values from -0.15625 to 0.15625
- out_weight: bfloat16 [768, 1536], P(('cfg', 'seq', 'rep')), may hold values from -0.21875 to 0.21875
Outputs:
- next_tokens: float32 [4, 4608, 1536], P('rep', 'seq', 'cfg')
Inputs may be any that keep to these rules, and one draw needn't show every extreme that they name: `text_lengths`: text tokens at or beyond the length are padding; some prompt of every draw has 154 valid tokens.
All inputs are finite; a program needn't handle non-finite values.
Results may differ from a plain program's by a relative error of at most 0.0044.
Values may be sent and summed in bfloat16 or wider, within the bound.
No kernel may reach another device: no remote copies, remote signals or barrier semaphores. Data moves between devices by JAX's collectives and lax.ppermute only.
A program may use at most 128 MiB of HBM per device.

v0:
```python
import jax
import jax.numpy as jnp
from jax import lax
from jax.sharding import PartitionSpec as P

HEADS = 12
HEAD_DIM = 64


def partner_2(x, axis, apart):
    return lax.ppermute(x, axis, [(i, i ^ 1 << apart) for i in range(lax.axis_size(axis))])


def layer_norm(values):
    row_mean = jnp.mean(values, axis=-1, keepdims=True)
    centred = values - row_mean
    row_var = jnp.mean(centred * centred, axis=-1, keepdims=True)
    return centred / jnp.sqrt(row_var + 1e-06)


def per_device(
    image_tokens,
    text_tokens,
    mod_image,
    mod_text,
    text_lengths,
    item_group,
    item_step,
    step_sizes,
    guide_scales,
    qkv_weight,
    kv_weight,
    out_weight,
):
    image_rows = image_tokens.shape[1]
    text_rows = text_tokens.shape[2]
    model_width = image_tokens.shape[2]
    heads_width = HEADS * HEAD_DIM
    picture = image_tokens[0]
    mod_one = mod_image[0, 0]
    mod_two = mod_text[0, 0]
    image_mod = (layer_norm(picture) * (1.0 + mod_one[1]) + mod_one[0]).astype(jnp.bfloat16)
    text_mod = (
        layer_norm(text_tokens[0, 0].astype(jnp.float32)) * (1.0 + mod_two[1]) + mod_two[0]
    ).astype(jnp.bfloat16)
    pieces = (
        lax.all_gather(qkv_weight, ("cfg", "seq", "rep"), axis=0, tiled=True),
        lax.all_gather(kv_weight, ("cfg", "seq", "rep"), axis=0, tiled=True),
    )
    qkv_total = jnp.dot(image_mod, pieces[0], preferred_element_type=jnp.float32)
    kv_total = jnp.dot(text_mod, pieces[1], preferred_element_type=jnp.float32)
    image_qkv = qkv_total.astype(jnp.bfloat16)
    text_kv = kv_total.astype(jnp.bfloat16)
    all_keys = jnp.concatenate(
        [image_qkv[:, heads_width : 2 * heads_width], text_kv[:, :heads_width]], axis=0
    )
    all_values = jnp.concatenate(
        [image_qkv[:, 2 * heads_width :], text_kv[:, heads_width:]], axis=0
    )
    queries = image_qkv[:, :heads_width].reshape(image_rows, HEADS, HEAD_DIM)
    length = text_lengths[0, 0]
    key_rows = image_rows + text_rows
    pieces = (
        lax.all_gather(all_keys, "seq", axis=0, tiled=True),
        lax.all_gather(all_values, "seq", axis=0, tiled=True),
    )
    running_max = jnp.full((HEADS, image_rows), -1e30, jnp.float32)
    piece_rows = pieces[0].shape[0]
    key_part = pieces[0].reshape(piece_rows, HEADS, HEAD_DIM)
    value_part = pieces[1].reshape(piece_rows, HEADS, HEAD_DIM)
    scores = (
        jnp.einsum("qhd,khd->hqk", queries, key_part, preferred_element_type=jnp.float32) * 0.125
    )
    key_index = jnp.arange(piece_rows, dtype=jnp.int32)
    key_owner = key_index // key_rows
    offset = key_index % key_rows
    usable_key = (offset < image_rows) | (key_owner * text_rows + offset - image_rows < length)
    scores = jnp.where(usable_key[None, None, :], scores, -1e30)
    new_max = jnp.maximum(running_max, jnp.max(scores, axis=-1))
    weights_now = jnp.exp(scores - new_max[:, :, None])
    row_total = jnp.sum(weights_now, axis=-1)
    weighted = jnp.einsum(
        "hqk,khd->hqd",
        weights_now.astype(jnp.bfloat16),
        value_part,
        preferred_element_type=jnp.float32,
    )
    running_max, row_total, weighted = (new_max, row_total, weighted)
    attended = (
        jnp.transpose(weighted / row_total[:, :, None], (1, 0, 2))
        .reshape(image_rows, heads_width)
        .astype(jnp.bfloat16)
    )
    projected = jnp.dot(
        attended,
        lax.all_gather(out_weight, ("cfg", "seq", "rep"), axis=0, tiled=True),
        preferred_element_type=jnp.float32,
    )
    velocity = mod_one[2] * projected
    half_width = model_width // 2
    cfg_index = lax.axis_index("cfg")
    guide_scale = jnp.sum(
        jnp.where(
            jnp.arange(guide_scales.shape[0], dtype=jnp.int32) == item_group[0], guide_scales, 0.0
        )
    )
    step_size = jnp.sum(
        jnp.where(jnp.arange(step_sizes.shape[0], dtype=jnp.int32) == item_step[0], step_sizes, 0.0)
    )
    partner = partner_2(velocity.astype(jnp.bfloat16), "cfg", 0).astype(velocity.dtype)
    cond_full = jnp.where(cfg_index == 0, velocity, partner)
    uncond_full = jnp.where(cfg_index == 0, partner, velocity)
    conditional = lax.dynamic_slice_in_dim(cond_full, cfg_index * half_width, half_width, 1)
    unconditional = lax.dynamic_slice_in_dim(uncond_full, cfg_index * half_width, half_width, 1)
    guided = unconditional + guide_scale * (conditional - unconditional)
    base_part = lax.dynamic_slice_in_dim(picture, cfg_index * half_width, half_width, 1)
    return (base_part + step_size * guided)[None]


def solution(mesh):
    placed = (
        P("rep", "seq", None),
        P("cfg", "rep", "seq", None),
        P("cfg", "rep", None, None),
        P("cfg", "rep", None, None),
        P("cfg", "rep"),
        P("rep"),
        P("rep"),
        P(),
        P(),
        P(("cfg", "seq", "rep"), None),
        P(("cfg", "seq", "rep"), None),
        P(("cfg", "seq", "rep"), None),
    )
    return jax.shard_map(
        per_device, mesh=mesh, in_specs=placed, out_specs=P("rep", "seq", "cfg"), check_vma=False
    )
```

profile of v0, /device:TPU:1, one launch (start us, length us, event | category | flops | bytes accessed | tf_op | source)
XLA Modules:
  0.0 1701.7 jit_solution(7112723287886544596)
XLA Ops:
  6.5 0.0 copy-start.1
  6.5 0.0 all-gather.13.cloned.1.call-start
  6.5 0.7 all-gather.13.cloned.1.call-update
  7.3 0.0 all-gather.11.cloned.1.call-start
  7.3 0.7 all-gather.11.cloned.1.call-update
  8.0 0.0 all-gather.19.cloned.1.call-start
  8.1 0.7 all-gather.19.cloned.1.call-update
  8.7 0.0 all-gather.17.cloned.1.call-start
  8.8 1.3 reduce_sum.64
  10.1 0.7 fusion.39
  10.8 0.9 convert_reduce_fusion
  11.7 0.7 slice_reduce_fusion.2
  12.4 0.8 add_reduce_fusion
  13.2 0.9 fusion.19
  14.2 1.4 multiply_reduce_fusion
  15.6 414.4 %all-gather.13.cloned.1.call-done = bf16[256,6,1536]{2,1,0:T(8,128)(2,1)} async-done(((bf16[1,6,1536]{2,1,0:T(8,128)(2,1)}), bf16[256,6,1536]{2,1,0:T(8,128)(2,1)}) %all-gather.13.cloned.1.call-update) | async-done | bytes 4718608 | tf_op jit(solution)/shard_map/all_gather | solution.py:48
  430.0 8.4 reshape.94
  438.4 0.0 copy-done.1
  438.4 3.1 convolution_convert_fusion.1
  441.5 0.0 copy-start
  441.5 410.2 %all-gather.11.cloned.1.call-done = bf16[256,6,2304]{2,1,0:T(8,128)(2,1)} async-done(((bf16[1,6,2304]{2,1,0:T(8,128)(2,1)}), bf16[256,6,2304]{2,1,0:T(8,128)(2,1)}) %all-gather.11.cloned.1.call-update) | async-done | bytes 7077904 | tf_op jit(solution)/shard_map/all_gather | solution.py:47
  851.6 11.6 reshape.92
  863.2 0.0 copy-done
  863.2 4.3 convolution_convert_fusion
  867.6 0.7 maximum_bitcast_fusion.1
  868.3 0.0 all-gather.17.cloned.1.call-update
  868.3 0.2 all-gather.15.cloned.1.call-start
  868.5 0.7 maximum_bitcast_fusion
  869.3 0.0 all-gather.15.cloned.1.call-update
  870.0 392.8 %all-gather.19.cloned.1.call-done = bf16[256,3,1536]{2,1,0:T(4,128)(2,1)} async-done(((bf16[1,3,1536]{2,1,0:T(4,128)(2,1)}), bf16[256,3,1536]{2,1,0:T(4,128)(2,1)}) %all-gather.19.cloned.1.call-update) | async-done | bytes 2359312 | tf_op jit(solution)/shard_map/all_gather | solution.py:96
  1262.7 5.3 reshape.100
  1268.1 0.9 copy.22
  1269.0 141.9 %all-gather.17.cloned.1.call-done = bf16[32,149,768]{2,1,0:T(8,128)(2,1)} async-done(((bf16[1,149,768]{2,1,0:T(8,128)(2,1)}), bf16[32,149,768]{2,1,0:T(8,128)(2,1)}) %all-gather.17.cloned.1.call-update) | async-done | bytes 7323664 | tf_op jit(solution)/shard_map/all_gather | solution.py:65
  1410.9 17.4 %copy.24 = bf16[32,149,768]{1,0,2:T(8,128)(2,1)} copy(bf16[32,149,768]{2,1,0:T(8,128)(2,1)} %all-gather.17.cloned.1.call-done) | data formatting | bytes 14647296 | tf_op jit(solution)/shard_map/all_gather | solution.py:65
  1428.4 20.8 %reshape.90 = bf16[4768,12,64]{0,2,1:T(8,128)(2,1)} reshape(bf16[32,149,768]{1,0,2:T(8,128)(2,1)} %copy.24) | data formatting | bytes 14647296 | tf_op jit(solution)/shard_map/reshape | solution.py:70
  1449.1 131.5 %all-gather.15.cloned.1.call-done = bf16[32,149,768]{2,1,0:T(8,128)(2,1)} async-done(((bf16[1,149,768]{2,1,0:T(8,128)(2,1)}), bf16[32,149,768]{2,1,0:T(8,128)(2,1)}) %all-gather.15.cloned.1.call-update) | async-done | bytes 7323664 | tf_op jit(solution)/shard_map/all_gather | solution.py:64
  1580.7 17.4 %copy.23 = bf16[32,149,768]{1,0,2:T(8,128)(2,1)} copy(bf16[32,149,768]{2,1,0:T(8,128)(2,1)} %all-gather.15.cloned.1.call-done) | data formatting | bytes 14647296 | tf_op jit(solution)/shard_map/all_gather | solution.py:64
  1598.1 20.8 %reshape.89 = bf16[4768,12,64]{0,2,1:T(8,128)(2,1)} reshape(bf16[32,149,768]{1,0,2:T(8,128)(2,1)} %copy.23) | data formatting | bytes 14647296 | tf_op jit(solution)/shard_map/reshape | solution.py:69
  1618.9 15.4 fusion
  1634.3 14.7 fusion.1
  1649.0 0.0 copy-start.2
  1649.0 0.0 copy-start.3
  1649.0 17.3 %divide_convert_fusion = bf16[144,12,64]{0,2,1:T(8,128)(2,1)} fusion(bf16[4768,12,64]{0,2,1:T(8,128)(2,1)} %reshape.90, f32[12,144,4768]{2,1,0:T(8,128)} %get-tuple-element.15, f32[12,144]{1,0:T(8,128)S(1)} %broadcast_maximum_fusion, pred[4768]{0:T(1024)(128)(4,1)S(1)} %fusion.38, f32[144,12]{0,1:T(8,128)S(1)} %bitcast.69), kind=kOutput, calls=%fused_computation.14 | convolution fusion | flops 1087782912 | bytes 40519840 | tf_op jit(solution)/shard_map/hqk,khd->hqd/dot_general | solution.py:82
  1666.3 2.6 fusion.46
  1668.9 20.6 %collective-permute-start = (bf16[144,1536]{1,0:T(8,128)(2,1)}, bf16[144,1536]{1,0:T(8,128)(2,1)S(1)}, u32[]{:S(2)}, u32[]{:S(2)}) collective-permute-start(bf16[144,1536]{1,0:T(8,128)(2,1)} %get-tuple-element.16), channel_id=1, source_target_pairs={{0,128},{128,0},{1,129},{129,1},{2,130},{130,2},{3,131},{131,3},{4... | collective-permute-start | bytes 1327112 | tf_op jit(solution)/shard_map/ppermute | solution.py:11
  1690.8 0.0 copy-done.2
  1690.8 0.6 fusion.41
  1691.4 0.0 copy-done.3
  1691.4 0.6 fusion.40
  1692.0 0.0 collective-permute-done
  1692.0 0.1 convert_element_type.43
  1692.1 3.1 fusion.11
  (8 shorter events, 0.1 us)
Async XLA Ops:
  6.5 431.8 %copy-start.1 = (bf16[1,1,5,1536]{3,2,1,0:T(8,128)(2,1)S(1)}, bf16[1,1,5,1536]{3,2,1,0:T(8,128)(2,1)}, u32[]{:S(2)}) copy-start(bf16[1,1,5,1536]{3,2,1,0:T(8,128)(2,1)} %param.13) | copy-start | bytes 46084
  6.5 423.4 %all-gather.13.cloned.1.call-start = ((), (), s32[]{:S(2)}) async-start(), calls=%async_computation.1 | async-start | bytes 6316032 | tf_op jit(solution)/shard_map/all_gather | solution.py:48
  7.3 844.4 %all-gather.11.cloned.1.call-start = ((), (), s32[]{:S(2)}) async-start(), calls=%async_computation | async-start | bytes 9474048 | tf_op jit(solution)/shard_map/all_gather | solution.py:47
  8.0 1254.7 %all-gather.19.cloned.1.call-start = ((), (), s32[]{:S(2)}) async-start(), calls=%async_computation.4 | async-start | bytes 3158016 | tf_op jit(solution)/shard_map/all_gather | solution.py:96
  8.7 1402.2 %all-gather.17.cloned.1.call-start = ((), (), s32[]{:S(2)}) async-start(), calls=%async_computation.3 | async-start | bytes 7704576 | tf_op jit(solution)/shard_map/all_gather | solution.py:65
  441.5 421.8 %copy-start = (f32[1,144,1536]{2,1,0:T(8,128)S(1)}, f32[1,144,1536]{2,1,0:T(8,128)}, u32[]{:S(2)}) copy-start(f32[1,144,1536]{2,1,0:T(8,128)} %param.12) | copy-start | bytes 2654212
  868.3 712.4 %all-gather.15.cloned.1.call-start = ((), (), s32[]{:S(2)}) async-start(), calls=%async_computation.2 | async-start | bytes 7704576 | tf_op jit(solution)/shard_map/all_gather | solution.py:64
  1649.0 41.8 %copy-start.2 = (f32[4]{0:T(128)S(1)}, f32[4]{0:T(128)}, u32[]{:S(2)}) copy-start(f32[4]{0:T(128)} %param.20) | copy-start | bytes 52
  1649.0 42.4 %copy-start.3 = (f32[28]{0:T(128)S(1)}, f32[28]{0:T(128)}, u32[]{:S(2)}) copy-start(f32[28]{0:T(128)} %param.19) | copy-start | bytes 340
  1668.9 23.1 %collective-permute-start = (bf16[144,1536]{1,0:T(8,128)(2,1)}, bf16[144,1536]{1,0:T(8,128)(2,1)S(1)}, u32[]{:S(2)}, u32[]{:S(2)}) collective-permute-start(bf16[144,1536]{1,0:T(8,128)(2,1)} %get-tuple-element.16), channel_id=1, source_target_pairs={{0,128},{128,0},{1,129},{129,1},{2,130},{130,2},{3,131},{131,3},{4... | collective-permute-start | bytes 1327112 | tf_op jit(solution)/shard_map/ppermute | solution.py:11
Sparse Core Ops, SparseCore 0:
  9.2 420.6 all-gather.12
  431.9 419.7 all-gather.10
  853.5 409.1 all-gather.18
  1264.4 146.5 all-gather.16
  1412.6 168.0 all-gather.14
where the time goes:
time: 1700 us
  waiting for transfers between devices  1490 us (88%)
  local copies, waits for them, and re-layouts  103 us (6%)
  matrix products  42.7 us (3%)
  other arithmetic  26.5 us (2%)
  starting transfers between devices  20.9 us (1%)
    all_gather x1, waiting for transfers between devices, per_device(): lax.all_gather(kv_weight, ('cfg', 'seq', 'rep'), axis=0, tiled=True)  414 us
    all_gather x1, waiting for transfers between devices, per_device(): lax.all_gather(qkv_weight, ('cfg', 'seq', 'rep'), axis=0, tiled=True)  410 us
    all_gather x1, waiting for transfers between devices, per_device(): lax.all_gather(out_weight, ('cfg', 'seq', 'rep'), axis=0, tiled=True)  393 us
    all_gather x1, waiting for transfers between devices, per_device(): lax.all_gather(all_values, 'seq', axis=0, tiled=True)  142 us
    all_gather x1, waiting for transfers between devices, per_device(): lax.all_gather(all_keys, 'seq', axis=0, tiled=True)  132 us
  transfers between devices with their start and end apart: 6, of which 5 were waited for; matrix products, arithmetic and copies ran while one was open for 5% of the time, Pallas kernels for 0%

commit v1 on v0

--- a/solution.py
+++ b/solution.py
@@ -9,6 +9,12 @@
 
 def partner_2(x, axis, apart):
     return lax.ppermute(x, axis, [(i, i ^ 1 << apart) for i in range(lax.axis_size(axis))])
+
+
+def gather_rows(flat, axes):
+    for axis in axes:
+        flat = lax.all_gather(flat, axis, axis=0)
+    return flat.reshape(-1, flat.shape[-1])
 
 
 def layer_norm(values):
@@ -43,12 +49,14 @@
     text_mod = (
         layer_norm(text_tokens[0, 0].astype(jnp.float32)) * (1.0 + mod_two[1]) + mod_two[0]
     ).astype(jnp.bfloat16)
-    pieces = (
-        lax.all_gather(qkv_weight, ("cfg", "seq", "rep"), axis=0, tiled=True),
-        lax.all_gather(kv_weight, ("cfg", "seq", "rep"), axis=0, tiled=True),
+    qkv_size = qkv_weight.size
+    joined = gather_rows(
+        jnp.concatenate([qkv_weight.reshape(-1), kv_weight.reshape(-1)]), ("rep", "seq", "cfg")
     )
-    qkv_total = jnp.dot(image_mod, pieces[0], preferred_element_type=jnp.float32)
-    kv_total = jnp.dot(text_mod, pieces[1], preferred_element_type=jnp.float32)
+    qkv_full = joined[:, :qkv_size].reshape(-1, qkv_weight.shape[1])
+    kv_full = joined[:, qkv_size:].reshape(-1, kv_weight.shape[1])
+    qkv_total = jnp.dot(image_mod, qkv_full, preferred_element_type=jnp.float32)
+    kv_total = jnp.dot(text_mod, kv_full, preferred_element_type=jnp.float32)
     image_qkv = qkv_total.astype(jnp.bfloat16)
     text_kv = kv_total.astype(jnp.bfloat16)
     all_keys = jnp.concatenate(
@@ -60,10 +68,8 @@
     queries = image_qkv[:, :heads_width].reshape(image_rows, HEADS, HEAD_DIM)
     length = text_lengths[0, 0]
     key_rows = image_rows + text_rows
-    pieces = (
-        lax.all_gather(all_keys, "seq", axis=0, tiled=True),
-        lax.all_gather(all_values, "seq", axis=0, tiled=True),
-    )
+    both = lax.all_gather(jnp.concatenate([all_keys, all_values], axis=1), "seq", axis=0, tiled=True)
+    pieces = (both[:, :heads_width], both[:, heads_width:])
     running_max = jnp.full((HEADS, image_rows), -1e30, jnp.float32)
     piece_rows = pieces[0].shape[0]
     key_part = pieces[0].reshape(piece_rows, HEADS, HEAD_DIM)
@@ -93,7 +99,7 @@
     )
     projected = jnp.dot(
         attended,
-        lax.all_gather(out_weight, ("cfg", "seq", "rep"), axis=0, tiled=True),
+        gather_rows(out_weight.reshape(-1), ("rep", "seq", "cfg")).reshape(-1, out_weight.shape[1]),
         preferred_element_type=jnp.float32,
     )
     velocity = mod_one[2] * projected

time: 1700 us -> 733 us (0.43)
  waiting for transfers between devices: 1490 us -> 507 us
  blocking collectives: 0 us -> 27.6 us
    all_gather x5, waiting for transfers between devices: 1490 us -> 507 us  [the longest x4 339 us: gather_rows(): flat = lax.all_gather(flat, axis, axis=0)]
    slice x1 -> x5, local copies, waits for them, and re-layouts: 0.05 us -> 42.2 us  [the longest x3 30.5 us: per_device(): pieces = (both[:, :heads_width], both[:, heads_width:])]
    all_gather x2 -> x0, local copies, waits for them, and re-layouts: 34.9 us -> none  [the longest x1 17.4 us: per_device(): lax.all_gather(all_values, 'seq', axis=0, tiled=True)]
    all_gather x0 -> x2, blocking collectives: none -> 27.6 us  [gather_rows(): flat = lax.all_gather(flat, axis, axis=0)]
    reshape x2 -> x5, local copies, waits for them, and re-layouts: 41.5 us -> 39.9 us  [the longest x1 15.6 us: gather_rows(): return flat.reshape(-1, flat.shape[-1])]
  transfers between devices with their start and end apart: 6 -> 6, of which waited for: 5 -> 4; matrix products, arithmetic and copies ran while one was open for 5% -> 9% of each run, Pallas kernels for 0% -> 0%
where the time goes in v1:
time: 733 us; the launch traced here: 731 us
  waiting for transfers between devices  507 us (69%)
  local copies, waits for them, and re-layouts  100 us (14%)
  matrix products  42.9 us (6%)
  blocking collectives  27.6 us (4%)
  other arithmetic  21.8 us (3%)
  starting transfers between devices  16 us (2%)
  between operations  15.3 us (2%)
    all_gather x4, waiting for transfers between devices, gather_rows(): flat = lax.all_gather(flat, axis, axis=0)  339 us
    all_gather x1, waiting for transfers between devices, per_device(): lax.all_gather(jnp.concatenate([all_keys, all_values], axis=1), 'seq', ax...  167 us
    slice x3, local copies, waits for them, and re-layouts, per_device(): pieces = (both[:, :heads_width], both[:, heads_width:])  30.5 us
    all_gather x2, blocking collectives, gather_rows(): flat = lax.all_gather(flat, axis, axis=0)  27.6 us
    dot_general x1, matrix products, per_device(): jnp.einsum('hqk,khd->hqd', weights_now.astype(jnp.bfloat16), value_part,...  17.5 us
    ppermute x1, starting transfers between devices, partner_2(): lax.ppermute(x, axis, [(i, i ^ 1 << apart) for i in range(lax.axis_size(a...  15.8 us
    reshape x1, local copies, waits for them, and re-layouts, gather_rows(): return flat.reshape(-1, flat.shape[-1])  15.6 us
    dot_general x1, matrix products, per_device(): jnp.einsum('qhd,khd->hqk', queries, key_part, preferred_element_type=jnp....  15.4 us
  transfers between devices with their start and end apart: 6, of which 4 were waited for; matrix products, arithmetic and copies ran while one was open for 9% of the time, Pallas kernels for 0%

profile of v1, /device:TPU:1, one launch (start us, length us, event | category | flops | bytes accessed | tf_op | source)
XLA Modules:
  0.0 730.9 jit_solution(8052315550756471500)
XLA Ops:
  6.5 0.0 copy-start
  6.5 0.0 copy-start.1
  6.5 0.0 copy-start.2
  6.5 0.0 copy-start.3
  6.5 0.0 all-gather.20.cloned.1.call-start
  6.6 0.9 reshape.157
  7.5 0.8 reshape.158
  8.3 0.1 reshape.172
  8.3 16.7 %all-gather.5 = bf16[4,1,23040]{2,1,0:T(2,128)(2,1)S(1)} all-gather(bf16[1,1,23040]{2,1,0:T(2,128)(2,1)S(1)} %reshape.172), channel_id=2, replica_groups=mesh['cfg'=2,'seq'=32,'rep'=4] {'rep'}, dimensions={0}, use_global_device_ids=true | all-gather | bytes 230400 | tf_op jit(solution)/shard_map/all_gather | solution.py:16
  25.1 0.8 copy.31
  25.9 0.0 all-gather.20.cloned.1.call-update
  25.9 0.0 all-gather.24.cloned.1.call-start
  25.9 0.7 reshape.178
  26.7 10.9 %all-gather.8 = bf16[4,1,4608]{2,1,0:T(2,128)(2,1)S(1)} all-gather(bf16[1,1,4608]{2,1,0:T(2,128)(2,1)S(1)} %reshape.178), channel_id=1, replica_groups=mesh['cfg'=2,'seq'=32,'rep'=4] {'rep'}, dimensions={0}, use_global_device_ids=true | all-gather | bytes 46080 | tf_op jit(solution)/shard_map/all_gather | solution.py:16
  37.5 0.6 copy.32
  38.1 0.0 all-gather.24.cloned.1.call-update
  38.2 0.0 all-gather.16.cloned.1.call-start
  38.2 136.4 %all-gather.20.cloned.1.call-done = bf16[32,4,23040]{2,1,0:T(4,128)(2,1)} async-done(((bf16[1,4,23040]{2,1,0:T(4,128)(2,1)}), bf16[32,4,23040]{2,1,0:T(4,128)(2,1)}) %all-gather.20.cloned.1.call-update) | async-done | bytes 5898256 | tf_op jit(solution)/shard_map/all_gather | solution.py:16
  174.6 0.0 all-gather.16.cloned.1.call-update
  174.6 0.0 all-gather.18.cloned.1.call-start
  174.7 1.3 reduce_sum.64
  176.0 0.0 copy-done.1
  176.0 0.1 convert_reduce_fusion
  176.1 0.0 copy-done.2
  176.1 0.0 copy-done.3
  176.2 150.9 %all-gather.24.cloned.1.call-done = bf16[32,4,4608]{2,1,0:T(4,128)(2,1)} async-done(((bf16[1,4,4608]{2,1,0:T(4,128)(2,1)}), bf16[32,4,4608]{2,1,0:T(4,128)(2,1)}) %all-gather.24.cloned.1.call-update) | async-done | bytes 1179664 | tf_op jit(solution)/shard_map/all_gather | solution.py:16
  327.2 0.0 all-gather.18.cloned.1.call-update
  327.2 0.0 all-gather.22.cloned.1.call-start
  327.3 0.2 fusion.24
  327.4 0.0 copy-done
  327.4 0.2 fusion.10
  327.7 52.1 %all-gather.16.cloned.1.call-done = bf16[64,4,23040]{2,1,0:T(4,128)(2,1)} async-done(((bf16[32,4,23040]{2,1,0:T(4,128)(2,1)}), bf16[64,4,23040]{2,1,0:T(4,128)(2,1)}) %all-gather.16.cloned.1.call-update) | async-done | bytes 11796496 | tf_op jit(solution)/shard_map/all_gather | solution.py:16
  379.8 15.6 %reshape.159 = bf16[256,23040]{1,0:T(8,128)(2,1)} reshape(bf16[64,4,23040]{2,1,0:T(4,128)(2,1)} %all-gather.16.cloned.1.call-done) | data formatting | bytes 23592960 | tf_op jit(solution)/shard_map/reshape | solution.py:17
  395.4 6.9 slice.61
  402.3 4.9 slice.64
  407.2 13.2 %reshape.160 = bf16[1536,2304]{1,0:T(8,128)(2,1)} reshape(bf16[256,13824]{1,0:T(8,128)(2,1)} %slice.61) | data formatting | bytes 14155776 | tf_op jit(solution)/shard_map/reshape | solution.py:56
  420.4 9.4 %reshape.162 = bf16[1536,1536]{1,0:T(8,128)(2,1)} reshape(bf16[256,9216]{1,0:T(8,128)(2,1)} %slice.64) | data formatting | bytes 9437184 | tf_op jit(solution)/shard_map/reshape | solution.py:57
  429.8 3.1 convolution_convert_fusion.1
  432.9 4.3 convolution_convert_fusion
  437.3 0.8 maximum_bitcast_fusion
  438.1 0.0 all-gather.22.cloned.1.call-update
  438.8 0.0 all-gather.18.cloned.1.call-done
  438.8 3.3 reshape_reshape.3
  442.1 0.9 copy.23
  443.0 167.3 %all-gather.22.cloned.1.call-done = bf16[32,149,1536]{2,1,0:T(8,128)(2,1)} async-done(((bf16[1,149,1536]{2,1,0:T(8,128)(2,1)}), bf16[32,149,1536]{2,1,0:T(8,128)(2,1)}) %all-gather.22.cloned.1.call-update) | async-done | bytes 14647312 | tf_op jit(solution)/shard_map/all_gather | solution.py:71
  610.4 11.9 %reshape.177 = bf16[4768,1536]{1,0:T(8,128)(2,1)} reshape(bf16[32,149,1536]{2,1,0:T(8,128)(2,1)} %all-gather.22.cloned.1.call-done) | data formatting | bytes 29294592
  622.3 10.4 %fusion.47 = (bf16[4768,768]{1,0:T(8,128)(2,1)}, bf16[4768,768]{1,0:T(8,128)(2,1)}) fusion(bf16[4768,1536]{1,0:T(8,128)(2,1)} %reshape.177), kind=kLoop, calls=%fused_computation.74 | loop fusion | bytes 29294592 | tf_op jit(solution)/shard_map/slice | solution.py:72
  632.7 10.0 %copy.24 = bf16[4768,768]{0,1:T(8,128)(2,1)} copy(bf16[4768,768]{1,0:T(8,128)(2,1)} %get-tuple-element.9) | data formatting | bytes 14647296 | tf_op jit(solution)/shard_map/slice | solution.py:72
  642.7 15.4 %fusion = (f32[12,144]{1,0:T(8,128)S(1)}, f32[12,144,4768]{2,1,0:T(8,128)}) fusion(pred[4768]{0:T(1024)(128)(4,1)S(1)} %fusion.41, bf16[144,12,64]{0,2,1:T(8,128)(2,1)} %bitcast.62, bf16[4768,12,64]{0,2,1:T(8,128)(2,1)} %bitcast.60), kind=kOutput, calls=%fused_computation.2 | convolution fusion | flops 1079320832 | bytes 40512928 | tf_op jit(solution)/shard_map/qhd,khd->hqk/dot_general | solution.py:78
  658.1 10.0 %copy.25 = bf16[4768,768]{0,1:T(8,128)(2,1)} copy(bf16[4768,768]{1,0:T(8,128)(2,1)} %get-tuple-element.10) | data formatting | bytes 14647296 | tf_op jit(solution)/shard_map/slice | solution.py:72
  668.2 14.7 %fusion.1 = f32[12,144]{1,0:T(8,128)S(1)} fusion(f32[12,144,4768]{2,1,0:T(8,128)} %get-tuple-element.17, f32[12,144]{1,0:T(8,128)S(1)} %broadcast_maximum_fusion, pred[4768]{0:T(1024)(128)(4,1)S(1)} %fusion.41), kind=kLoop, calls=%fused_computation.3 | loop fusion | flops 32954688 | bytes 32975008 | tf_op jit(solution)/shard_map/reduce_sum | solution.py:87
  682.8 0.0 copy-start.4
  682.8 0.0 copy-start.5
  682.8 17.5 %divide_convert_fusion = bf16[144,12,64]{0,2,1:T(8,128)(2,1)} fusion(bf16[4768,12,64]{0,2,1:T(8,128)(2,1)} %bitcast.61, f32[12,144,4768]{2,1,0:T(8,128)} %get-tuple-element.17, f32[12,144]{1,0:T(8,128)S(1)} %broadcast_maximum_fusion, pred[4768]{0:T(1024)(128)(4,1)S(1)} %fusion.41, f32[144,12]{0,1:T(8,128)S(1)} %bitcast.66), kind=kOutput, calls=%fused_computation.15 | convolution fusion | flops 1087782912 | bytes 40519840 | tf_op jit(solution)/shard_map/hqk,khd->hqd/dot_general | solution.py:88
  700.4 2.6 fusion.50
  703.0 15.8 %collective-permute-start = (bf16[144,1536]{1,0:T(8,128)(2,1)}, bf16[144,1536]{1,0:T(8,128)(2,1)S(1)}, u32[]{:S(2)}, u32[]{:S(2)}) collective-permute-start(bf16[144,1536]{1,0:T(8,128)(2,1)} %get-tuple-element.18), channel_id=1, source_target_pairs={{0,128},{128,0},{1,129},{129,1},{2,130},{130,2},{3,131},{131,3},{4... | collective-permute-start | bytes 1327112 | tf_op jit(solution)/shard_map/ppermute | solution.py:11
  720.0 0.0 copy-done.4
  720.0 0.6 fusion.43
  720.6 0.0 copy-done.5
  720.6 0.6 fusion.44
  721.2 0.0 collective-permute-done
  721.2 0.1 convert_element_type.52
  721.3 3.1 fusion.14
  (12 shorter events, 0.2 us)
Async XLA Ops:
  6.5 320.9 %copy-start = (f32[1,144,1536]{2,1,0:T(8,128)S(1)}, f32[1,144,1536]{2,1,0:T(8,128)}, u32[]{:S(2)}) copy-start(f32[1,144,1536]{2,1,0:T(8,128)} %param.12) | copy-start | bytes 2654212
  6.5 169.4 %copy-start.1 = (bf16[1,1,5,1536]{3,2,1,0:T(8,128)(2,1)S(1)}, bf16[1,1,5,1536]{3,2,1,0:T(8,128)(2,1)}, u32[]{:S(2)}) copy-start(bf16[1,1,5,1536]{3,2,1,0:T(8,128)(2,1)} %param.13) | copy-start | bytes 46084
  6.5 169.6 %copy-start.2 = (f32[1,1,3,1536]{3,1,2,0:T(1,128)S(1)}, f32[1,1,3,1536]{3,1,2,0:T(1,128)}, u32[]{:S(2)}) copy-start(f32[1,1,3,1536]{3,1,2,0:T(1,128)} %param.14) | copy-start | bytes 55300
  6.5 169.6 %copy-start.3 = (f32[1,1,2,1536]{3,2,1,0:T(2,128)S(1)}, f32[1,1,2,1536]{3,2,1,0:T(2,128)}, u32[]{:S(2)}) copy-start(f32[1,1,2,1536]{3,2,1,0:T(2,128)} %param.15) | copy-start | bytes 36868
  6.5 168.1 %all-gather.20.cloned.1.call-start = ((), (), s32[]{:S(2)}) async-start(), calls=%async_computation.2 | async-start | bytes 6082560 | tf_op jit(solution)/shard_map/all_gather | solution.py:16
  25.9 301.3 %all-gather.24.cloned.1.call-start = ((), (), s32[]{:S(2)}) async-start(), calls=%async_computation.4 | async-start | bytes 1216512 | tf_op jit(solution)/shard_map/all_gather | solution.py:16
  38.2 341.7 %all-gather.16.cloned.1.call-start = ((), (), s32[]{:S(2)}) async-start(), calls=%async_computation | async-start | bytes 17694720 | tf_op jit(solution)/shard_map/all_gather | solution.py:16
  174.6 264.2 %all-gather.18.cloned.1.call-start = ((), (), s32[]{:S(2)}) async-start(), calls=%async_computation.1 | async-start | bytes 3538944 | tf_op jit(solution)/shard_map/all_gather | solution.py:16
  327.2 283.2 %all-gather.22.cloned.1.call-start = ((), (), s32[]{:S(2)}) async-start(), calls=%async_computation.3 | async-start | bytes 15409152 | tf_op jit(solution)/shard_map/all_gather | solution.py:71
  682.8 37.2 %copy-start.4 = (f32[28]{0:T(128)S(1)}, f32[28]{0:T(128)}, u32[]{:S(2)}) copy-start(f32[28]{0:T(128)} %param.19) | copy-start | bytes 340
  682.8 37.8 %copy-start.5 = (f32[4]{0:T(128)S(1)}, f32[4]{0:T(128)}, u32[]{:S(2)}) copy-start(f32[4]{0:T(128)} %param.20) | copy-start | bytes 52
  703.0 18.3 %collective-permute-start = (bf16[144,1536]{1,0:T(8,128)(2,1)}, bf16[144,1536]{1,0:T(8,128)(2,1)S(1)}, u32[]{:S(2)}, u32[]{:S(2)}) collective-permute-start(bf16[144,1536]{1,0:T(8,128)(2,1)} %get-tuple-element.18), channel_id=1, source_target_pairs={{0,128},{128,0},{1,129},{129,1},{2,130},{130,2},{3,131},{131,3},{4... | collective-permute-start | bytes 1327112 | tf_op jit(solution)/shard_map/ppermute | solution.py:11
Sparse Core Ops, SparseCore 0:
  26.0 148.5 all-gather.19
  176.4 150.7 all-gather.23
  329.0 50.8 all-gather.15
  381.5 17.5 all-gather.17
  438.2 172.1 all-gather.21
